TPU v7x, 512 devices: a whole 4x4x16 slice. The times are simulated.
512 devices in a mesh: expert: 128 (over x, z, core), dp: 4 (over y).
Axes of the slice: x: 4, y: 4, z: 16, core: 2. Of those that a mesh axis runs over, the one named last changes fastest.
Arguments:
- tokens: bfloat16 [16384, 3584], P('expert', 'dp'), may hold values from -6 to 6
- route_ids: int32 [16384, 8], P('expert'), may hold values from 0 to 127, as said below
- gate_scores: float32 [16384, 8], P('expert'), may hold values from 0.1 to 1, as said below
- up_weight: bfloat16 [128, 3584, 1024], P('expert', 'dp'), may hold values from -0.09375 to 0.09375
- down_weight: bfloat16 [128, 1024, 3584], P('expert', None, 'dp'), may hold values from -0.1875 to 0.1875
Outputs:
- mixed: bfloat16 [16384, 3584], P('expert', 'dp')
Inputs may be any that keep to these rules, and one draw needn't show every extreme that they name: `route_ids`: each row names 8 different experts. The same 2 experts are named by exactly 15 rows in every aligned block of 128 rows (the tokens of one device); in such a block every other expert is named by 8 - 1 or 8 rows. `gate_scores`: positive affinities.
All inputs are finite; a program needn't handle non-finite values.
Results may differ from a plain program's by a relative error of at most 0.017.
Values may be sent and summed in bfloat16 or wider, within the bound.
No kernel may reach another device: no remote copies, remote signals or barrier semaphores. Data moves between devices by JAX's collectives and lax.ppermute only.
A program may use at most 64 MiB of HBM per device.

v0:
```python
import jax
import jax.numpy as jnp
from jax import lax
from jax.sharding import PartitionSpec as P

HOT = 2
CHUNKS = 3
ROUTE_SCALE = 2.5


def silu_hidden(before):
    summed = lax.psum(before.astype(jnp.bfloat16), "dp").astype(jnp.float32)
    result = jax.nn.silu(summed).astype(jnp.bfloat16)
    return result


def expert_chunk(piece, up_local, down_local, previous):
    experts, item_count, features = piece.shape
    arrived = lax.all_to_all(piece, "expert", split_axis=0, concat_axis=0, tiled=True)
    flat_rows = arrived.reshape(-1, features)
    before = jnp.dot(flat_rows, up_local, preferred_element_type=jnp.float32)
    if previous is not None:
        before, previous = lax.optimization_barrier((before, previous))
    hidden = silu_hidden(before)
    output = jnp.dot(hidden, down_local, preferred_element_type=jnp.float32)
    outcome = output.astype(jnp.bfloat16).reshape(experts, item_count, features)
    returned = lax.all_to_all(outcome, "expert", split_axis=0, concat_axis=0, tiled=True)
    return (returned, hidden)


def local(tokens, route_ids, gate_scores, up_weight, down_weight):
    token_count, chosen_count = route_ids.shape
    features = tokens.shape[1]
    experts = lax.axis_size("expert")
    mean_rows = token_count * chosen_count // experts
    hot_most = min(2 * mean_rows - 1, token_count)
    cold_rows = (experts - HOT) * mean_rows - HOT * (hot_most - mean_rows)
    cold_most = -(-cold_rows // (experts - HOT))
    flat_ids = route_ids.reshape(-1)
    row_total = flat_ids.shape[0]
    expert_range = jnp.arange(experts, dtype=jnp.int32)
    onehot = (flat_ids[:, None] == expert_range[None, :]).astype(jnp.int32)
    running = jnp.cumsum(onehot, axis=0) - 1
    row_ranks = jnp.sum(onehot * running, axis=1)
    padded = jnp.concatenate([tokens, jnp.zeros((1, features), tokens.dtype)], axis=0)
    up_local = up_weight[0]
    down_local = down_weight[0]
    mix_weights = gate_scores * (ROUTE_SCALE / jnp.sum(gate_scores, axis=1, keepdims=True))
    slot_count = max(hot_most, cold_most)
    slot_of_row = flat_ids * slot_count + row_ranks
    slot_table = jnp.full((experts * slot_count,), row_total, jnp.int32)
    slot_table = slot_table.at[slot_of_row].set(jnp.arange(row_total, dtype=jnp.int32), mode="drop")
    sending = padded[slot_table // chosen_count].reshape(experts, slot_count, features)
    bounds = [slot_count * c // CHUNKS for c in range(CHUNKS + 1)]
    pieces = []
    previous = None
    for lo, hi in zip(bounds[:-1], bounds[1:]):
        returned, previous = expert_chunk(sending[:, lo:hi], up_local, down_local, previous)
        pieces.append(returned)
    returned = jnp.concatenate(pieces, axis=1).reshape(-1, features)
    picked = returned[slot_of_row]
    picked = picked.reshape(token_count, chosen_count, features).astype(jnp.float32)
    mixed = jnp.sum(mix_weights[:, :, None] * picked, axis=1)
    return mixed.astype(jnp.bfloat16)


def solution(mesh):
    return jax.shard_map(
        local,
        mesh=mesh,
        in_specs=(
            P("expert", "dp"),
            P("expert", None),
            P("expert", None),
            P("expert", "dp", None),
            P("expert", None, "dp"),
        ),
        out_specs=P("expert", "dp"),
        check_vma=False,
    )
```

profile of v0, /device:TPU:1, one launch (start us, length us, event | category | flops | bytes accessed | tf_op | source)
XLA Modules:
  0.0 652.5 jit_solution(6864148417399794794)
XLA Ops:
  6.5 0.0 copy-start
  6.5 0.9 copy.9
  7.5 0.0 copy-start.1
  7.5 0.1 eq.29
  7.6 0.1 eq.25
  7.6 0.7 broadcast_multiply_fusion
  8.3 0.1 copy.11
  8.4 0.2 fusion.40
  8.7 0.1 copy.12
  8.8 0.1 copy.8
  8.9 0.1 mul.50
  9.0 0.4 fusion.39
  9.4 4.3 scatter_custom_fusion
  13.8 0.0 copy-done.1
  13.8 7.1 %gather_fusion = bf16[1920,896]{1,0:T(8,128)(2,1)} fusion(bf16[129,896]{1,0:T(8,128)(2,1)S(1)} %concatenate.6, s32[2048]{0:T(1024)S(1)} %pad_clamp_fusion), kind=kCustom, calls=%fused_computation | custom fusion | bytes 6888960 | tf_op jit(solution)/shard_map/gather | solution.py:53
  21.0 5.7 reshape.81
  26.7 5.4 fusion.48
  32.1 108.1 %all_to_all.30 = bf16[128,5,896]{2,1,0:T(8,128)(2,1)} all-to-all(bf16[128,5,896]{2,1,0:T(8,128)(2,1)S(1)} %get-tuple-element.9), channel_id=1, replica_groups=mesh['expert'=128,'dp'=4] {'expert'}, dimensions={0} | all-to-all | bytes 2293760 | tf_op jit(solution)/shard_map/all_to_all | solution.py:19
  140.2 96.5 %all_to_all.31 = bf16[128,5,896]{2,1,0:T(8,128)(2,1)} all-to-all(bf16[128,5,896]{2,1,0:T(8,128)(2,1)S(1)} %get-tuple-element.11), channel_id=1, replica_groups=mesh['expert'=128,'dp'=4] {'expert'}, dimensions={0} | all-to-all | bytes 2293760 | tf_op jit(solution)/shard_map/all_to_all | solution.py:19
  236.7 9.1 %all-to-all-start.4 = ((bf16[128,5,896]{2,1,0:T(8,128)(2,1)}), bf16[128,5,896]{2,1,0:T(8,128)(2,1)}, u32[]{:S(2)}, u32[]{:S(2)}) async-start(bf16[128,5,896]{2,1,0:T(8,128)(2,1)} %get-tuple-element.10), calls=%async_computation.4 | async-start | bytes 3670016 | tf_op jit(solution)/shard_map/all_to_all | solution.py:19
  245.8 0.2 all-reduce.5.cloned.1.call-start
  246.1 2.5 reshape.82
  248.5 0.0 copy-done
  248.6 2.6 fusion.25
  251.1 0.0 all-reduce.5.cloned.1.call-update
  251.2 63.4 %all-reduce.5.cloned.1.call-done = bf16[640,1024]{1,0:T(8,128)(2,1)} async-done(((bf16[640,1024]{1,0:T(8,128)(2,1)}), bf16[640,1024]{1,0:T(8,128)(2,1)}) %all-reduce.5.cloned.1.call-update) | async-done | bytes 1310736 | tf_op jit(solution)/shard_map/psum | solution.py:12
  314.6 0.0 copy-start.3
  314.6 2.2 fusion.4
  316.8 0.0 copy-done.3
  316.8 1.5 fusion.28
  318.3 1.5 reshape.83
  319.8 13.6 %all-to-all-done.4 = bf16[128,5,896]{2,1,0:T(8,128)(2,1)} async-done(((bf16[128,5,896]{2,1,0:T(8,128)(2,1)}), bf16[128,5,896]{2,1,0:T(8,128)(2,1)}, u32[]{:S(2)}, u32[]{:S(2)}) %all-to-all-start.4) | async-done | bytes 1146912 | tf_op jit(solution)/shard_map/all_to_all | solution.py:19
  333.4 9.1 %all-to-all-start.1 = ((bf16[128,5,896]{2,1,0:T(8,128)(2,1)}), bf16[128,5,896]{2,1,0:T(8,128)(2,1)}, u32[]{:S(2)}, u32[]{:S(2)}) async-start(bf16[128,5,896]{2,1,0:T(8,128)(2,1)} %reshape.83), calls=%async_computation.1 | async-start | bytes 3670016 | tf_op jit(solution)/shard_map/all_to_all | solution.py:27
  342.5 0.0 all-reduce.7.cloned.1.call-start
  342.6 2.5 reshape.84
  345.1 2.6 fusion.21
  347.7 0.0 all-reduce.7.cloned.1.call-update
  347.7 63.4 %all-reduce.7.cloned.1.call-done = bf16[640,1024]{1,0:T(8,128)(2,1)} async-done(((bf16[640,1024]{1,0:T(8,128)(2,1)}), bf16[640,1024]{1,0:T(8,128)(2,1)}) %all-reduce.7.cloned.1.call-update) | async-done | bytes 1310736 | tf_op jit(solution)/shard_map/psum | solution.py:12
  411.1 0.0 copy-start.4
  411.1 2.2 fusion.8
  413.3 0.0 copy-done.4
  413.3 1.5 fusion.31
  414.9 1.5 reshape.85
  416.3 13.8 %all-to-all-done.1 = bf16[128,5,896]{2,1,0:T(8,128)(2,1)} async-done(((bf16[128,5,896]{2,1,0:T(8,128)(2,1)}), bf16[128,5,896]{2,1,0:T(8,128)(2,1)}, u32[]{:S(2)}, u32[]{:S(2)}) %all-to-all-start.1) | async-done | bytes 1146912 | tf_op jit(solution)/shard_map/all_to_all | solution.py:27
  430.1 9.1 %all-to-all-start.3 = ((bf16[128,5,896]{2,1,0:T(8,128)(2,1)}), bf16[128,5,896]{2,1,0:T(8,128)(2,1)}, u32[]{:S(2)}, u32[]{:S(2)}) async-start(bf16[128,5,896]{2,1,0:T(8,128)(2,1)} %reshape.85), calls=%async_computation.3 | async-start | bytes 3670016 | tf_op jit(solution)/shard_map/all_to_all | solution.py:27
  439.2 0.3 all-reduce.9.cloned.1.call-start
  439.5 2.5 reshape.86
  442.0 2.6 fusion.19
  444.6 0.0 all-reduce.9.cloned.1.call-update
  444.6 63.4 %all-reduce.9.cloned.1.call-done = bf16[640,1024]{1,0:T(8,128)(2,1)} async-done(((bf16[640,1024]{1,0:T(8,128)(2,1)}), bf16[640,1024]{1,0:T(8,128)(2,1)}) %all-reduce.9.cloned.1.call-update) | async-done | bytes 1310736 | tf_op jit(solution)/shard_map/psum | solution.py:12
  508.0 3.4 fusion.34
  511.5 1.5 reshape.87
  513.0 0.0 copy-start.2
  513.0 13.8 %all-to-all-done.3 = bf16[128,5,896]{2,1,0:T(8,128)(2,1)} async-done(((bf16[128,5,896]{2,1,0:T(8,128)(2,1)}), bf16[128,5,896]{2,1,0:T(8,128)(2,1)}, u32[]{:S(2)}, u32[]{:S(2)}) %all-to-all-start.3) | async-done | bytes 1146912 | tf_op jit(solution)/shard_map/all_to_all | solution.py:27
  526.8 9.1 %all-to-all-start.5 = ((bf16[128,5,896]{2,1,0:T(8,128)(2,1)}), bf16[128,5,896]{2,1,0:T(8,128)(2,1)}, u32[]{:S(2)}, u32[]{:S(2)}) async-start(bf16[128,5,896]{2,1,0:T(8,128)(2,1)} %reshape.87), calls=%async_computation.5 | async-start | bytes 3670016 | tf_op jit(solution)/shard_map/all_to_all | solution.py:27
  535.9 0.0 copy-done.2
  536.0 0.1 copy.7
  536.1 87.4 %all-to-all-done.5 = bf16[128,5,896]{2,1,0:T(8,128)(2,1)} async-done(((bf16[128,5,896]{2,1,0:T(8,128)(2,1)}), bf16[128,5,896]{2,1,0:T(8,128)(2,1)}, u32[]{:S(2)}, u32[]{:S(2)}) %all-to-all-start.5) | async-done | bytes 1146912 | tf_op jit(solution)/shard_map/all_to_all | solution.py:27
  623.5 5.3 pad_maximum_fusion
  628.8 5.7 reshape.88
  634.5 8.1 %gather_fusion.1 = bf16[1024,896]{1,0:T(8,128)(2,1)} fusion(bf16[1920,896]{1,0:T(8,128)(2,1)} %reshape.88, s32[1024]{0:T(1024)S(1)} %broadcast_clamp_fusion), kind=kCustom, calls=%fused_computation.1 | custom fusion | bytes 3674112 | tf_op jit(solution)/shard_map/gather | solution.py:61
  642.6 3.4 fusion
  (13 shorter events, 0.2 us)
Async XLA Ops:
  6.5 242.0 %copy-start = (bf16[1,896,1024]{2,1,0:T(8,128)(2,1)S(1)}, bf16[1,896,1024]{2,1,0:T(8,128)(2,1)}, u32[]{:S(2)}) copy-start(bf16[1,896,1024]{2,1,0:T(8,128)(2,1)} %param.8) | copy-start | bytes 5505028
  7.5 6.3 copy-start.1
  236.7 96.7 %all-to-all-start.4 = ((bf16[128,5,896]{2,1,0:T(8,128)(2,1)}), bf16[128,5,896]{2,1,0:T(8,128)(2,1)}, u32[]{:S(2)}, u32[]{:S(2)}) async-start(bf16[128,5,896]{2,1,0:T(8,128)(2,1)} %get-tuple-element.10), calls=%async_computation.4 | async-start | bytes 3670016 | tf_op jit(solution)/shard_map/all_to_all | solution.py:19
  245.8 68.7 %all-reduce.5.cloned.1.call-start = ((), (), s32[]{:S(2)}) async-start(), calls=%async_computation.6 | async-start | bytes 2621440 | tf_op jit(solution)/shard_map/psum | solution.py:12
  314.6 2.2 copy-start.3
  333.4 96.7 %all-to-all-start.1 = ((bf16[128,5,896]{2,1,0:T(8,128)(2,1)}), bf16[128,5,896]{2,1,0:T(8,128)(2,1)}, u32[]{:S(2)}, u32[]{:S(2)}) async-start(bf16[128,5,896]{2,1,0:T(8,128)(2,1)} %reshape.83), calls=%async_computation.1 | async-start | bytes 3670016 | tf_op jit(solution)/shard_map/all_to_all | solution.py:27
  342.5 68.6 %all-reduce.7.cloned.1.call-start = ((), (), s32[]{:S(2)}) async-start(), calls=%async_computation.7 | async-start | bytes 2621440 | tf_op jit(solution)/shard_map/psum | solution.py:12
  411.1 2.2 copy-start.4
  430.1 96.7 %all-to-all-start.3 = ((bf16[128,5,896]{2,1,0:T(8,128)(2,1)}), bf16[128,5,896]{2,1,0:T(8,128)(2,1)}, u32[]{:S(2)}, u32[]{:S(2)}) async-start(bf16[128,5,896]{2,1,0:T(8,128)(2,1)} %reshape.85), calls=%async_computation.3 | async-start | bytes 3670016 | tf_op jit(solution)/shard_map/all_to_all | solution.py:27
  439.2 68.8 %all-reduce.9.cloned.1.call-start = ((), (), s32[]{:S(2)}) async-start(), calls=%async_computation.8 | async-start | bytes 2621440 | tf_op jit(solution)/shard_map/psum | solution.py:12
  513.0 23.0 %copy-start.2 = (f32[128,8]{0,1:T(8,128)S(1)}, f32[128,8]{0,1:T(8,128)}, u32[]{:S(2)}) copy-start(f32[128,8]{0,1:T(8,128)} %param.7) | copy-start | bytes 12292
  526.8 96.7 %all-to-all-start.5 = ((bf16[128,5,896]{2,1,0:T(8,128)(2,1)}), bf16[128,5,896]{2,1,0:T(8,128)(2,1)}, u32[]{:S(2)}, u32[]{:S(2)}) async-start(bf16[128,5,896]{2,1,0:T(8,128)(2,1)} %reshape.87), calls=%async_computation.5 | async-start | bytes 3670016 | tf_op jit(solution)/shard_map/all_to_all | solution.py:27
Sparse Core Ops, SparseCore 0:
  251.3 63.2 all-reduce.4
  347.8 63.2 all-reduce.6
  444.7 63.2 all-reduce.8
where the time goes:
time: 654 us; the launch traced here: 653 us
  waiting for transfers between devices  319 us (49%)
  blocking collectives  205 us (31%)
  local copies, waits for them, and re-layouts  50 us (8%)
  starting transfers between devices  37 us (6%)
  other arithmetic  14.5 us (2%)
  matrix products  14.3 us (2%)
  between operations  13.4 us (2%)
    all_to_all x2, blocking collectives, expert_chunk(): lax.all_to_all(piece, 'expert', split_axis=0, concat_axis=0, tiled=True)  205 us
    psum x3, waiting for transfers between devices, silu_hidden(): summed = lax.psum(before.astype(jnp.bfloat16), 'dp').astype(jnp.float32)  190 us
    all_to_all x3, waiting for transfers between devices, expert_chunk(): lax.all_to_all(outcome, 'expert', split_axis=0, concat_axis=0, tiled=True)  115 us
    all_to_all x3, starting transfers between devices, expert_chunk(): lax.all_to_all(outcome, 'expert', split_axis=0, concat_axis=0, tiled=True)  27.4 us
    all_to_all x1, waiting for transfers between devices, expert_chunk(): lax.all_to_all(piece, 'expert', split_axis=0, concat_axis=0, tiled=True)  13.6 us
  transfers between devices with their start and end apart: 7, of which 7 were waited for; matrix products, arithmetic and copies ran while one was open for 5% of the time, Pallas kernels for 0%

commit v1 on v0

--- a/solution.py
+++ b/solution.py
@@ -2,6 +2,7 @@
 import jax.numpy as jnp
 from jax import lax
 from jax.sharding import PartitionSpec as P
+from jax.lax import all_gather
 
 HOT = 2
 CHUNKS = 3
@@ -9,7 +10,7 @@
 
 
 def silu_hidden(before):
-    summed = lax.psum(before.astype(jnp.bfloat16), "dp").astype(jnp.float32)
+    summed = all_gather(before.astype(jnp.bfloat16), axis_name="dp").sum(axis=0).astype(jnp.float32)
     result = jax.nn.silu(summed).astype(jnp.bfloat16)
     return result
 

time: 654 us -> 682 us (1.043)
  blocking collectives: 205 us -> 302 us
  waiting for transfers between devices: 319 us -> 239 us
  other arithmetic: 14.5 us -> 24.8 us
  starting transfers between devices: 37 us -> 27.4 us
    psum x3 -> x0, waiting for transfers between devices: 190 us -> none  [silu_hidden(): summed = lax.psum(before.astype(jnp.bfloat16), 'dp').astype(jnp.float32)]
    all_to_all x3, waiting for transfers between devices: 115 us -> 239 us  [expert_chunk(): lax.all_to_all(outcome, 'expert', split_axis=0, concat_axis=0, tiled=True)]
    all_to_all x2 -> x3, blocking collectives: 205 us -> 302 us  [expert_chunk(): lax.all_to_all(piece, 'expert', split_axis=0, concat_axis=0, tiled=True)]
    all_to_all x1 -> x0, waiting for transfers between devices: 13.6 us -> none  [expert_chunk(): lax.all_to_all(piece, 'expert', split_axis=0, concat_axis=0, tiled=True)]
    reduce_sum x0 -> x3, other arithmetic: none -> 12.3 us  [silu_hidden(): all_gather(before.astype(jnp.bfloat16), axis_name='dp').sum(axis=0)]
    all_to_all x1 -> x0, starting transfers between devices: 9.13 us -> none  [expert_chunk(): lax.all_to_all(piece, 'expert', split_axis=0, concat_axis=0, tiled=True)]
  transfers between devices with their start and end apart: 7 -> 6, of which waited for: 7 -> 3; matrix products, arithmetic and copies ran while one was open for 5% -> 6% of each run, Pallas kernels for 0% -> 0%
where the time goes in v1:
time: 682 us; the launch traced here: 680 us
  blocking collectives  302 us (44%)
  waiting for transfers between devices  239 us (35%)
  local copies, waits for them, and re-layouts  55.3 us (8%)
  starting transfers between devices  27.4 us (4%)
  other arithmetic  24.8 us (4%)
  matrix products  18.9 us (3%)
  between operations  13.3 us (2%)
    all_to_all x3, blocking collectives, expert_chunk(): lax.all_to_all(piece, 'expert', split_axis=0, concat_axis=0, tiled=True)  302 us
    all_to_all x3, waiting for transfers between devices, expert_chunk(): lax.all_to_all(outcome, 'expert', split_axis=0, concat_axis=0, tiled=True)  239 us
    all_to_all x3, starting transfers between devices, expert_chunk(): lax.all_to_all(outcome, 'expert', split_axis=0, concat_axis=0, tiled=True)  27.1 us
  transfers between devices with their start and end apart: 6, of which 3 were waited for; matrix products, arithmetic and copies ran while one was open for 6% of the time, Pallas kernels for 0%

profile of v1, /device:TPU:1, one launch (start us, length us, event | category | flops | bytes accessed | tf_op | source)
XLA Modules:
  0.0 680.3 jit_solution(17452881831499892103)
XLA Ops:
  6.5 0.0 copy-start
  6.5 0.0 all-gather.7.cloned.1.call-start
  6.5 0.8 broadcast_multiply_fusion
  7.4 0.8 copy.9
  8.1 0.0 copy-start.4
  8.2 0.1 eq.29
  8.2 0.1 eq.25
  8.3 0.1 copy.8
  8.4 0.1 mul.50
  8.5 0.1 copy.11
  8.6 0.2 fusion.40
  8.9 0.1 copy.12
  9.0 0.4 fusion.39
  9.4 4.3 scatter_custom_fusion
  13.8 0.0 copy-done.4
  13.8 7.1 %gather_fusion = bf16[1920,896]{1,0:T(8,128)(2,1)} fusion(bf16[129,896]{1,0:T(8,128)(2,1)S(1)} %concatenate.6, s32[2048]{0:T(1024)S(1)} %pad_clamp_fusion), kind=kCustom, calls=%fused_computation | custom fusion | bytes 6888960 | tf_op jit(solution)/shard_map/gather | solution.py:54
  21.0 5.7 reshape.81
  26.7 6.0 fusion.48
  32.7 108.1 %all_to_all.30 = bf16[128,5,896]{2,1,0:T(8,128)(2,1)} all-to-all(bf16[128,5,896]{2,1,0:T(8,128)(2,1)S(1)} %get-tuple-element.9), channel_id=1, replica_groups=mesh['expert'=128,'dp'=4] {'expert'}, dimensions={0} | all-to-all | bytes 2293760 | tf_op jit(solution)/shard_map/all_to_all | solution.py:20
  140.8 2.5 reshape.82
  143.3 0.0 copy-done
  143.3 2.6 fusion.25
  145.9 0.0 all-gather.7.cloned.1.call-update
  145.9 0.0 all-gather.9.cloned.1.call-start
  146.0 96.7 %all_to_all.31 = bf16[128,5,896]{2,1,0:T(8,128)(2,1)} all-to-all(bf16[128,5,896]{2,1,0:T(8,128)(2,1)} %get-tuple-element.11), channel_id=1, replica_groups=mesh['expert'=128,'dp'=4] {'expert'}, dimensions={0} | all-to-all | bytes 2293760 | tf_op jit(solution)/shard_map/all_to_all | solution.py:20
  242.7 2.5 reshape.84
  245.1 2.6 fusion.21
  247.8 0.0 all-gather.7.cloned.1.call-done
  247.8 4.1 reduce_sum.68
  251.9 1.8 fusion.4
  253.7 0.0 all-gather.9.cloned.1.call-update
  253.7 96.7 %all_to_all.32 = bf16[128,5,896]{2,1,0:T(8,128)(2,1)} all-to-all(bf16[128,5,896]{2,1,0:T(8,128)(2,1)} %get-tuple-element.10), channel_id=1, replica_groups=mesh['expert'=128,'dp'=4] {'expert'}, dimensions={0} | all-to-all | bytes 2293760 | tf_op jit(solution)/shard_map/all_to_all | solution.py:20
  350.4 0.0 copy-start.2
  350.4 3.6 reshape.86
  354.0 0.0 copy-done.2
  354.0 4.0 fusion.28
  358.0 3.3 reshape.83
  361.3 0.0 copy-start.3
  361.3 9.3 %all-to-all-start.1 = ((bf16[128,5,896]{2,1,0:T(8,128)(2,1)}), bf16[128,5,896]{2,1,0:T(8,128)(2,1)}, u32[]{:S(2)}, u32[]{:S(2)}) async-start(bf16[128,5,896]{2,1,0:T(8,128)(2,1)} %reshape.83), calls=%async_computation.1 | async-start | bytes 3670016 | tf_op jit(solution)/shard_map/all_to_all | solution.py:28
  370.6 0.3 all-gather.11.cloned.1.call-start
  370.8 0.0 copy-done.3
  370.9 2.6 fusion.19
  373.4 0.0 all-gather.9.cloned.1.call-done
  373.4 4.1 reduce_sum.69
  377.5 0.8 fusion.8
  378.3 0.0 all-gather.11.cloned.1.call-update
  378.3 3.0 fusion.31
  381.4 1.5 reshape.85
  382.9 75.3 %all-to-all-done.1 = bf16[128,5,896]{2,1,0:T(8,128)(2,1)} async-done(((bf16[128,5,896]{2,1,0:T(8,128)(2,1)}), bf16[128,5,896]{2,1,0:T(8,128)(2,1)}, u32[]{:S(2)}, u32[]{:S(2)}) %all-to-all-start.1) | async-done | bytes 1146912 | tf_op jit(solution)/shard_map/all_to_all | solution.py:28
  458.1 8.7 %all-to-all-start.3 = ((bf16[128,5,896]{2,1,0:T(8,128)(2,1)}), bf16[128,5,896]{2,1,0:T(8,128)(2,1)S(1)}, u32[]{:S(2)}, u32[]{:S(2)}) async-start(bf16[128,5,896]{2,1,0:T(8,128)(2,1)} %reshape.85), calls=%async_computation.3 | async-start | bytes 3670016 | tf_op jit(solution)/shard_map/all_to_all | solution.py:28
  466.9 0.0 all-gather.11.cloned.1.call-done
  466.9 4.1 reduce_sum.70
  471.0 4.0 fusion.34
  475.1 3.3 reshape.87
  478.3 76.4 %all-to-all-done.3 = bf16[128,5,896]{2,1,0:T(8,128)(2,1)S(1)} async-done(((bf16[128,5,896]{2,1,0:T(8,128)(2,1)}), bf16[128,5,896]{2,1,0:T(8,128)(2,1)S(1)}, u32[]{:S(2)}, u32[]{:S(2)}) %all-to-all-start.3) | async-done | bytes 1146912 | tf_op jit(solution)/shard_map/all_to_all | solution.py:28
  554.7 9.1 %all-to-all-start.5 = ((bf16[128,5,896]{2,1,0:T(8,128)(2,1)}), bf16[128,5,896]{2,1,0:T(8,128)(2,1)}, u32[]{:S(2)}, u32[]{:S(2)}) async-start(bf16[128,5,896]{2,1,0:T(8,128)(2,1)} %reshape.87), calls=%async_computation.5 | async-start | bytes 3670016 | tf_op jit(solution)/shard_map/all_to_all | solution.py:28
  563.9 0.0 copy-done.5
  563.9 0.1 copy.7
  564.0 87.4 %all-to-all-done.5 = bf16[128,5,896]{2,1,0:T(8,128)(2,1)} async-done(((bf16[128,5,896]{2,1,0:T(8,128)(2,1)}), bf16[128,5,896]{2,1,0:T(8,128)(2,1)}, u32[]{:S(2)}, u32[]{:S(2)}) %all-to-all-start.5) | async-done | bytes 1146912 | tf_op jit(solution)/shard_map/all_to_all | solution.py:28
  651.4 5.0 pad_maximum_fusion
  656.4 5.7 reshape.88
  662.1 8.3 %gather_fusion.1 = bf16[1024,896]{1,0:T(8,128)(2,1)} fusion(bf16[1920,896]{1,0:T(8,128)(2,1)} %reshape.88, s32[1024]{0:T(1024)S(1)} %broadcast_clamp_fusion), kind=kCustom, calls=%fused_computation.1 | custom fusion | bytes 3674112 | tf_op jit(solution)/shard_map/gather | solution.py:62
  670.4 3.4 fusion
  673.8 0.0 copy-done.1
  (15 shorter events, 0.2 us)
Async XLA Ops:
  6.5 136.8 %copy-start = (bf16[1,896,1024]{2,1,0:T(8,128)(2,1)S(1)}, bf16[1,896,1024]{2,1,0:T(8,128)(2,1)}, u32[]{:S(2)}) copy-start(bf16[1,896,1024]{2,1,0:T(8,128)(2,1)} %param.8) | copy-start | bytes 5505028
  6.5 241.2 %all-gather.7.cloned.1.call-start = ((), (), s32[]{:S(2)}) async-start(), calls=%async_computation.6 | async-start | bytes 6553600 | tf_op jit(solution)/shard_map/all_gather | solution.py:13
  8.1 5.7 copy-start.4
  145.9 227.5 %all-gather.9.cloned.1.call-start = ((), (), s32[]{:S(2)}) async-start(), calls=%async_computation.7 | async-start | bytes 6553600 | tf_op jit(solution)/shard_map/all_gather | solution.py:13
  350.4 3.6 copy-start.2
  361.3 9.5 %copy-start.3 = (bf16[640,896]{1,0:T(8,128)(2,1)S(1)}, bf16[640,896]{1,0:T(8,128)(2,1)}, u32[]{:S(2)}) copy-start(bf16[640,896]{1,0:T(8,128)(2,1)} %reshape.86) | copy-start | bytes 3440644
  361.3 96.8 %all-to-all-start.1 = ((bf16[128,5,896]{2,1,0:T(8,128)(2,1)}), bf16[128,5,896]{2,1,0:T(8,128)(2,1)}, u32[]{:S(2)}, u32[]{:S(2)}) async-start(bf16[128,5,896]{2,1,0:T(8,128)(2,1)} %reshape.83), calls=%async_computation.1 | async-start | bytes 3670016 | tf_op jit(solution)/shard_map/all_to_all | solution.py:28
  370.6 96.3 %all-gather.11.cloned.1.call-start = ((), (), s32[]{:S(2)}) async-start(), calls=%async_computation.8 | async-start | bytes 6553600 | tf_op jit(solution)/shard_map/all_gather | solution.py:13
  458.1 96.6 %all-to-all-start.3 = ((bf16[128,5,896]{2,1,0:T(8,128)(2,1)}), bf16[128,5,896]{2,1,0:T(8,128)(2,1)S(1)}, u32[]{:S(2)}, u32[]{:S(2)}) async-start(bf16[128,5,896]{2,1,0:T(8,128)(2,1)} %reshape.85), calls=%async_computation.3 | async-start | bytes 3670016 | tf_op jit(solution)/shard_map/all_to_all | solution.py:28
  478.3 85.5 %copy-start.5 = (f32[128,8]{0,1:T(8,128)S(1)}, f32[128,8]{0,1:T(8,128)}, u32[]{:S(2)}) copy-start(f32[128,8]{0,1:T(8,128)} %param.7) | copy-start | bytes 12292
  554.7 96.7 %all-to-all-start.5 = ((bf16[128,5,896]{2,1,0:T(8,128)(2,1)}), bf16[128,5,896]{2,1,0:T(8,128)(2,1)}, u32[]{:S(2)}, u32[]{:S(2)}) async-start(bf16[128,5,896]{2,1,0:T(8,128)(2,1)} %reshape.87), calls=%async_computation.5 | async-start | bytes 3670016 | tf_op jit(solution)/shard_map/all_to_all | solution.py:28
  662.1 11.7 %copy-start.1 = (bf16[1,896,1024]{2,1,0:T(8,128)(2,1)S(1)}, bf16[1,896,1024]{2,1,0:T(8,128)(2,1)}, u32[]{:S(2)}) copy-start(bf16[1,896,1024]{2,1,0:T(8,128)(2,1)} %param.8) | copy-start | bytes 5505028
Sparse Core Ops, SparseCore 0:
  146.0 58.0 all-gather.6
  253.8 58.0 all-gather.8
  378.5 65.5 all-gather.10
